TPU v7x, 32 devices: a whole 2x2x4 slice. The times are simulated.
32 devices in a mesh: grp: 1, tok: 32 (over z, y, x, core).
Axes of the slice: x: 2, y: 2, z: 4, core: 2. Of those that a mesh axis runs over, the one named last changes fastest.
Arguments:
- activations: bfloat16 [65536, 2048], P('tok')
- out_grads: bfloat16 [65536, 512], P('tok')
- v_bank: bfloat16 [2048, 65536], P('tok'), may hold values from -0.125 to 0.125
- u_bank: bfloat16 [512, 65536], P('tok'), may hold values from -0.25 to 0.25
- query_ids: int32 [16], P('grp'), may hold values from 0 to 2047, as said below
Outputs:
- influence: float32 [65536, 16], P('tok', 'grp')
Inputs may be any that keep to these rules, and one draw needn't show every extreme that they name: `query_ids`: the ids are distinct; both 0 and 2047 are among them.
All inputs are finite; a program needn't handle non-finite values.
Results may differ from a plain program's by a relative error of at most 0.0003.
Values may be sent and summed in bfloat16 or wider, within the bound.
No kernel may reach another device: no remote copies, remote signals or barrier semaphores. Data moves between devices by JAX's collectives and lax.ppermute only.
A program may use at most 128 MiB of HBM per device.

v0:
```python
import jax
import jax.numpy as jnp
from jax import lax
from jax.sharding import PartitionSpec as P

RANK = 32


def select_columns(bank, query_ids):
    pieces = [
        lax.dynamic_slice_in_dim(bank, query_ids[q] * RANK, RANK, axis=1)
        for q in range(query_ids.shape[0])
    ]
    return jnp.concatenate(pieces, axis=1)


def folder(left, piece):
    return jnp.dot(left, piece, preferred_element_type=jnp.float32)


def total_over(x, axis):
    n = lax.axis_size(axis)
    copies = jnp.broadcast_to(x[None], (n,) + x.shape)
    return lax.all_to_all(copies, axis, 0, 0, tiled=False).sum(axis=0)


def on_device(activations, out_grads, v_bank, u_bank, query_ids):
    tok_rows = activations.shape[0]
    queries = query_ids.shape[0]
    v_sel = select_columns(v_bank, query_ids)
    u_sel = select_columns(u_bank, query_ids)
    proj_in = folder(activations, lax.all_gather(v_sel, "tok", axis=0, tiled=True))
    proj_out = folder(out_grads, lax.all_gather(u_sel, "tok", axis=0, tiled=True))
    scores = (proj_in * proj_out).reshape(tok_rows, queries, RANK).sum(axis=2)
    total = total_over(jnp.sum(scores * scores, axis=0), "tok")
    count = tok_rows * lax.axis_size("tok")
    scale = jnp.sqrt(total / count + 1e-06)
    return scores / scale[None, :]


def solution(mesh):
    return jax.shard_map(
        on_device,
        mesh=mesh,
        in_specs=(P("tok", None), P("tok", None), P("tok", None), P("tok", None), P("grp")),
        out_specs=P("tok", "grp"),
        check_vma=False,
    )
```

profile of v0, /device:TPU:0, one launch (start us, length us, event | category | flops | bytes accessed | tf_op | source)
XLA Modules:
  0.0 108.0 jit_solution(6873853208284179090)
XLA Ops:
  6.5 0.0 copy-start
  6.5 0.0 all-gather.2.cloned.1.call-start
  6.5 2.0 %fusion = (s32[1]{0:T(128)}, s32[1]{0:T(128)}, s32[1]{0:T(128)}, s32[1]{0:T(128)}, s32[1]{0:T(128)}, /*index=5*/s32[1]{0:T(128)}, s32[1]{0:T(128)}, s32[1]{0:T(1...) fusion(s32[16]{0:T(128)} %param.9), kind=kLoop, calls=%fused_computation.37 | loop fusion | bytes 128 | tf_op jit(solution)/shard_map/slice | solution.py:11
  18.6 1.1 %constant_dynamic-slice_fusion.16 = (bf16[64,32]{1,0:T(8,128)(2,1)S(1)}, bf16[64,32]{1,0:T(8,128)(2,1)S(1)}, bf16[64,32]{1,0:T(8,128)(2,1)S(1)}, bf16[64,32]{1,0...) fusion(bf16[64,65536]{1,0:T(8,128)(2,1)} %param.7, ...), kind=kLoop, calls=%fused_computation.20 | loop fusion | bytes 131136 | tf_op jit(solution)/shard_map/dynamic_slice | solution.py:11
  19.7 0.8 concatenate.6
  20.5 0.0 all-gather.2.cloned.1.call-update
  20.5 1.0 constant_dynamic-slice_fusion
  21.5 0.1 concatenate.7
  21.7 45.0 %all_gather.7 = bf16[512,512]{1,0:T(8,128)(2,1)S(1)} all-gather(bf16[16,512]{1,0:T(8,128)(2,1)S(1)} %concatenate.7), channel_id=1, replica_groups=mesh['grp'=1,'tok'=32] {'tok'}, dimensions={0}, use_global_device_ids=true | all-gather | bytes 540672 | tf_op jit(solution)/shard_map/all_gather | solution.py:33
  66.6 0.0 copy-done
  66.7 3.2 %fusion.1 = f32[512,2048]{1,0:T(8,128)} fusion(bf16[512,512]{1,0:T(8,128)(2,1)S(1)} %all_gather.7, bf16[2048,512]{1,0:T(8,128)(2,1)S(1)} %copy-done), kind=kOutput, calls=%fused_computation.38 | convolution fusion | flops 1073741824 | bytes 6815744 | tf_op jit(solution)/shard_map/dot_general | solution.py:18
  69.9 10.1 %all-gather.2.cloned.1.call-done = bf16[2048,512]{1,0:T(8,128)(2,1)} async-done(((bf16[64,512]{1,0:T(8,128)(2,1)}), bf16[2048,512]{1,0:T(8,128)(2,1)}) %all-gather.2.cloned.1.call-update) | async-done | bytes 2097168 | tf_op jit(solution)/shard_map/all_gather | solution.py:32
  80.0 9.8 %bitcast_reduce_fusion = f32[2048,16]{0,1:T(8,128)S(1)} fusion(f32[512,2048]{1,0:T(8,128)} %fusion.1, bf16[2048,512]{1,0:T(8,128)(2,1)} %all-gather.2.cloned.1.call-done, bf16[2048,2048]{1,0:T(8,128)(2,1)} %param.5), kind=kOutput, calls=%fused_computation | convolution fusion | flops 4297031680 | bytes 14811136 | tf_op jit(solution)/shard_map/dot_general | solution.py:18
  89.8 0.1 multiply_reduce_fusion
  89.9 10.4 %all_to_all.6 = f32[32,1,16]{2,1,0:T(1,128)S(1)} all-to-all(f32[32,1,16]{2,1,0:T(1,128)S(1)} %broadcast_in_dim.2), channel_id=1, replica_groups=mesh['grp'=1,'tok'=32] {'tok'}, dimensions={0} | all-to-all | bytes 4096 | tf_op jit(solution)/shard_map/all_to_all | solution.py:24
  100.3 0.1 reduce_sum.29
  100.4 0.7 broadcast_divide_fusion
  (2 shorter events, 0.0 us)
Async XLA Ops:
  6.5 60.1 %copy-start = (bf16[2048,512]{1,0:T(8,128)(2,1)S(1)}, bf16[2048,512]{1,0:T(8,128)(2,1)}, u32[]{:S(2)}) copy-start(bf16[2048,512]{1,0:T(8,128)(2,1)} %param.6) | copy-start | bytes 6291460
  6.5 73.5 %all-gather.2.cloned.1.call-start = ((), (), s32[]{:S(2)}) async-start(), calls=%async_computation.1 | async-start | bytes 2162688 | tf_op jit(solution)/shard_map/all_gather | solution.py:32
Sparse Core Ops, SparseCore 0:
  20.6 59.3 all-gather.1
where the time goes:
time: 108 us
  blocking collectives  55.4 us (51%)
  between operations  23.5 us (22%)
  matrix products  13 us (12%)
  waiting for transfers between devices  10.1 us (9%)
  local copies, waits for them, and re-layouts  4.99 us (5%)
    all_gather x1, blocking collectives, on_device(): lax.all_gather(u_sel, 'tok', axis=0, tiled=True)  45 us
    dot_general x2, matrix products, folder(): return jnp.dot(left, piece, preferred_element_type=jnp.float32)  13 us
    all_to_all x1, blocking collectives, total_over(): return lax.all_to_all(copies, axis, 0, 0, tiled=False).sum(axis=0)  10.4 us
    all_gather x1, waiting for transfers between devices, on_device(): lax.all_gather(v_sel, 'tok', axis=0, tiled=True)  10.1 us
  transfers between devices with their start and end apart: 1, of which 1 were waited for; matrix products, arithmetic and copies ran while one was open for 4% of the time, Pallas kernels for 0%

commit v1 on v0

--- a/solution.py
+++ b/solution.py
@@ -4,6 +4,27 @@
 from jax.sharding import PartitionSpec as P
 
 RANK = 32
+
+
+def joined_along(blocks, dim):
+    dims = list(blocks.shape[1:])
+    dims[dim] *= blocks.shape[0]
+    return jnp.moveaxis(blocks, 0, dim).reshape(dims)
+
+
+def doubled(x, axis):
+    size, index = (lax.axis_size(axis), lax.axis_index(axis))
+    tiles, bit = (x[None], 1)
+    while bit < size:
+        other = lax.ppermute(tiles, axis, [(i, i ^ bit) for i in range(size)])
+        low = index & bit == 0
+        tiles = jnp.concatenate([jnp.where(low, tiles, other), jnp.where(low, other, tiles)])
+        bit *= 2
+    return tiles
+
+
+def collect(x, axis, dim):
+    return joined_along(doubled(x, axis), dim)
 
 
 def select_columns(bank, query_ids):
@@ -29,7 +50,7 @@
     queries = query_ids.shape[0]
     v_sel = select_columns(v_bank, query_ids)
     u_sel = select_columns(u_bank, query_ids)
-    proj_in = folder(activations, lax.all_gather(v_sel, "tok", axis=0, tiled=True))
+    proj_in = folder(activations, collect(v_sel, "tok", 0))
     proj_out = folder(out_grads, lax.all_gather(u_sel, "tok", axis=0, tiled=True))
     scores = (proj_in * proj_out).reshape(tok_rows, queries, RANK).sum(axis=2)
     total = total_over(jnp.sum(scores * scores, axis=0), "tok")

time: 108 us -> 142 us (1.31)
  blocking collectives: 55.4 us -> 80.7 us
  between operations: 23.5 us -> 10.3 us
  waiting for transfers between devices: 10.1 us -> 22 us
  starting transfers between devices: 0.01 us -> 9.01 us
  other arithmetic: 0.94 us -> 4.9 us
  matrix products: 13 us -> 9.83 us
    all_gather x1, blocking collectives: 45 us -> 69.4 us  [on_device(): lax.all_gather(u_sel, 'tok', axis=0, tiled=True)]
    ppermute x0 -> x5, waiting for transfers between devices: none -> 22 us  [doubled(): other = lax.ppermute(tiles, axis, [(i, i ^ bit) for i in range(size)])]
    all_gather x1 -> x0, waiting for transfers between devices: 10.1 us -> none  [on_device(): lax.all_gather(v_sel, 'tok', axis=0, tiled=True)]
    ppermute x0 -> x5, starting transfers between devices: none -> 9.01 us  [doubled(): other = lax.ppermute(tiles, axis, [(i, i ^ bit) for i in range(size)])]
    dot_general x2, matrix products: 13 us -> 9.83 us  [folder(): return jnp.dot(left, piece, preferred_element_type=jnp.float32)]
    select_n x0 -> x5, other arithmetic: none -> 2.63 us  [doubled(): jnp.where(low, tiles, other)]
  transfers between devices with their start and end apart: 1 -> 5, of which waited for: 1 -> 4; matrix products, arithmetic and copies ran while one was open for 4% -> 2% of each run, Pallas kernels for 0% -> 0%
where the time goes in v1:
time: 142 us
  blocking collectives  80.7 us (57%)
  waiting for transfers between devices  22 us (15%)
  between operations  10.3 us (7%)
  matrix products  9.83 us (7%)
  starting transfers between devices  9.01 us (6%)
  local copies, waits for them, and re-layouts  4.97 us (4%)
  other arithmetic  4.9 us (3%)
    all_gather x1, blocking collectives, on_device(): lax.all_gather(u_sel, 'tok', axis=0, tiled=True)  69.4 us
    ppermute x5, waiting for transfers between devices, doubled(): other = lax.ppermute(tiles, axis, [(i, i ^ bit) for i in range(size)])  22 us
    all_to_all x1, blocking collectives, total_over(): return lax.all_to_all(copies, axis, 0, 0, tiled=False).sum(axis=0)  11.2 us
    dot_general x2, matrix products, folder(): return jnp.dot(left, piece, preferred_element_type=jnp.float32)  9.83 us
    ppermute x5, starting transfers between devices, doubled(): other = lax.ppermute(tiles, axis, [(i, i ^ bit) for i in range(size)])  9.01 us
  transfers between devices with their start and end apart: 5, of which 4 were waited for; matrix products, arithmetic and copies ran while one was open for 2% of the time, Pallas kernels for 0%

profile of v1, /device:TPU:0, one launch (start us, length us, event | category | flops | bytes accessed | tf_op | source)
XLA Modules:
  0.0 141.6 jit_solution(13341683843244450950)
XLA Ops:
  0.0 0.0 copy-start
  0.0 2.0 %fusion = (s32[1]{0:T(128)}, s32[1]{0:T(128)}, s32[1]{0:T(128)}, s32[1]{0:T(128)}, s32[1]{0:T(128)}, /*index=5*/s32[1]{0:T(128)}, s32[1]{0:T(128)}, s32[1]{0:T(1...) fusion(s32[16]{0:T(128)} %param.9), kind=kLoop, calls=%fused_computation.52 | loop fusion | bytes 128 | tf_op jit(solution)/shard_map/slice | solution.py:32
  12.1 1.1 constant_dynamic-slice_fusion.16
  13.2 0.1 concatenate.21
  13.4 0.5 collective-permute-start
  13.9 0.9 collective-permute-done
  14.9 2.9 %collective-permute-start.1 = (bf16[2,64,512]{2,1,0:T(8,128)(2,1)S(1)}, bf16[2,64,512]{2,1,0:T(8,128)(2,1)S(1)}, u32[]{:S(2)}, u32[]{:S(2)}) collective-permute-start(bf16[2,64,512]{2,1,0:T(8,128)(2,1)S(1)} %pad_maximum_fusion.4), channel_id=1, source_target_pairs={{0,2},{1,3},{2,0},{3,1},{4,6},{5,7},{6,4},{7,5},{8,10},{9,11},{10,... | collective-permute-start | bytes 393224 | tf_op jit(solution)/shard_map/ppermute | solution.py:19
  17.8 3.8 %collective-permute-done.1 = bf16[2,64,512]{2,1,0:T(8,128)(2,1)S(1)} collective-permute-done((bf16[2,64,512]{2,1,0:T(8,128)(2,1)S(1)}, bf16[2,64,512]{2,1,0:T(8,128)(2,1)S(1)}, u32[]{:S(2)}, u32[]{:S(2)}) %collective-permute-start.1) | collective-permute-done | bytes 131104 | tf_op jit(solution)/shard_map/ppermute | solution.py:19
  21.6 1.8 %collective-permute-start.2 = (bf16[4,64,512]{2,1,0:T(8,128)(2,1)S(1)}, bf16[4,64,512]{2,1,0:T(8,128)(2,1)S(1)}, u32[]{:S(2)}, u32[]{:S(2)}) collective-permute-start(bf16[4,64,512]{2,1,0:T(8,128)(2,1)S(1)} %pad_maximum_fusion.3), channel_id=1, source_target_pairs={{0,4},{1,5},{2,6},{3,7},{4,0},{5,1},{6,2},{7,3},{8,12},{9,13},{10,... | collective-permute-start | bytes 786440 | tf_op jit(solution)/shard_map/ppermute | solution.py:19
  23.5 6.1 %collective-permute-done.2 = bf16[4,64,512]{2,1,0:T(8,128)(2,1)S(1)} collective-permute-done((bf16[4,64,512]{2,1,0:T(8,128)(2,1)S(1)}, bf16[4,64,512]{2,1,0:T(8,128)(2,1)S(1)}, u32[]{:S(2)}, u32[]{:S(2)}) %collective-permute-start.2) | collective-permute-done | bytes 262176 | tf_op jit(solution)/shard_map/ppermute | solution.py:19
  29.6 0.0 copy-start.1
  29.6 0.7 copy-done.1
  30.4 1.6 %collective-permute-start.3 = (bf16[8,64,512]{2,1,0:T(8,128)(2,1)S(1)}, bf16[8,64,512]{2,1,0:T(8,128)(2,1)}, u32[]{:S(2)}, u32[]{:S(2)}) collective-permute-start(bf16[8,64,512]{2,1,0:T(8,128)(2,1)S(1)} %pad_maximum_fusion.2), channel_id=1, source_target_pairs={{0,8},{1,9},{2,10},{3,11},{4,12},{5,13},{6,14},{7,15},{8,0},{9,1},... | collective-permute-start | bytes 1572872 | tf_op jit(solution)/shard_map/ppermute | solution.py:19
  31.9 11.2 %collective-permute-done.3 = bf16[8,64,512]{2,1,0:T(8,128)(2,1)} collective-permute-done((bf16[8,64,512]{2,1,0:T(8,128)(2,1)S(1)}, bf16[8,64,512]{2,1,0:T(8,128)(2,1)}, u32[]{:S(2)}, u32[]{:S(2)}) %collective-permute-start.3) | collective-permute-done | bytes 524320 | tf_op jit(solution)/shard_map/ppermute | solution.py:19
  43.1 1.2 broadcast_select_fusion.3
  44.3 1.1 pad_maximum_fusion.1
  45.3 2.2 %collective-permute-start.4 = (bf16[16,64,512]{2,1,0:T(8,128)(2,1)}, bf16[16,64,512]{2,1,0:T(8,128)(2,1)}, u32[]{:S(2)}, u32[]{:S(2)}) collective-permute-start(bf16[16,64,512]{2,1,0:T(8,128)(2,1)} %pad_maximum_fusion.1), channel_id=1, source_target_pairs={{0,16},{1,17},{2,18},{3,19},{4,20},{5,21},{6,22},{7,23},{8,24},{9,... | collective-permute-start | bytes 3145736 | tf_op jit(solution)/shard_map/ppermute | solution.py:19
  47.5 0.9 constant_dynamic-slice_fusion
  48.5 0.1 concatenate.27
  48.6 69.4 %all_gather.3 = bf16[512,512]{1,0:T(8,128)(2,1)S(1)} all-gather(bf16[16,512]{1,0:T(8,128)(2,1)S(1)} %concatenate.27), channel_id=1, replica_groups=mesh['grp'=1,'tok'=32] {'tok'}, dimensions={0}, use_global_device_ids=true | all-gather | bytes 540672 | tf_op jit(solution)/shard_map/all_gather | solution.py:54
  118.0 0.0 copy-done
  118.0 1.3 fusion.1
  119.3 0.0 collective-permute-done.4
  119.3 1.4 broadcast_select_fusion.1
  120.7 0.2 pad_maximum_fusion
  120.9 8.5 %bitcast_reduce_fusion = f32[2048,16]{0,1:T(8,128)S(1)} fusion(f32[512,2048]{1,0:T(8,128)S(1)} %fusion.1, bf16[2048,512]{1,0:T(8,128)(2,1)S(1)} %bitcast.28, bf16[2048,2048]{1,0:T(8,128)(2,1)} %param.5), kind=kOutput, calls=%fused_computation | convolution fusion | flops 4297031680 | bytes 14811136 | tf_op jit(solution)/shard_map/dot_general | solution.py:39
  129.4 0.1 multiply_reduce_fusion
  129.6 11.2 %all_to_all.6 = f32[32,1,16]{2,1,0:T(1,128)S(1)} all-to-all(f32[32,1,16]{2,1,0:T(1,128)S(1)} %broadcast_in_dim.5), channel_id=1, replica_groups=mesh['grp'=1,'tok'=32] {'tok'}, dimensions={0} | all-to-all | bytes 4096 | tf_op jit(solution)/shard_map/all_to_all | solution.py:45
  140.8 0.1 reduce_sum.29
  140.9 0.7 broadcast_divide_fusion
  (8 shorter events, 0.2 us)
Async XLA Ops:
  0.0 118.0 %copy-start = (bf16[2048,512]{1,0:T(8,128)(2,1)S(1)}, bf16[2048,512]{1,0:T(8,128)(2,1)}, u32[]{:S(2)}) copy-start(bf16[2048,512]{1,0:T(8,128)(2,1)} %param.6) | copy-start | bytes 6291460
  13.4 1.4 %collective-permute-start = (bf16[1,64,512]{2,1,0:T(8,128)(2,1)S(1)}, bf16[1,64,512]{2,1,0:T(8,128)(2,1)S(1)}, u32[]{:S(2)}, u32[]{:S(2)}) collective-permute-start(bf16[1,64,512]{2,1,0:T(8,128)(2,1)S(1)} %bitcast.29), channel_id=1, source_target_pairs={{0,1},{1,0},{2,3},{3,2},{4,5},{5,4},{6,7},{7,6},{8,9},{9,8},{10,11... | collective-permute-start | bytes 196616 | tf_op jit(solution)/shard_map/ppermute | solution.py:19
  14.9 6.7 %collective-permute-start.1 = (bf16[2,64,512]{2,1,0:T(8,128)(2,1)S(1)}, bf16[2,64,512]{2,1,0:T(8,128)(2,1)S(1)}, u32[]{:S(2)}, u32[]{:S(2)}) collective-permute-start(bf16[2,64,512]{2,1,0:T(8,128)(2,1)S(1)} %pad_maximum_fusion.4), channel_id=1, source_target_pairs={{0,2},{1,3},{2,0},{3,1},{4,6},{5,7},{6,4},{7,5},{8,10},{9,11},{10,... | collective-permute-start | bytes 393224 | tf_op jit(solution)/shard_map/ppermute | solution.py:19
  21.6 7.9 %collective-permute-start.2 = (bf16[4,64,512]{2,1,0:T(8,128)(2,1)S(1)}, bf16[4,64,512]{2,1,0:T(8,128)(2,1)S(1)}, u32[]{:S(2)}, u32[]{:S(2)}) collective-permute-start(bf16[4,64,512]{2,1,0:T(8,128)(2,1)S(1)} %pad_maximum_fusion.3), channel_id=1, source_target_pairs={{0,4},{1,5},{2,6},{3,7},{4,0},{5,1},{6,2},{7,3},{8,12},{9,13},{10,... | collective-permute-start | bytes 786440 | tf_op jit(solution)/shard_map/ppermute | solution.py:19
  29.6 0.7 copy-start.1
  30.4 12.7 %collective-permute-start.3 = (bf16[8,64,512]{2,1,0:T(8,128)(2,1)S(1)}, bf16[8,64,512]{2,1,0:T(8,128)(2,1)}, u32[]{:S(2)}, u32[]{:S(2)}) collective-permute-start(bf16[8,64,512]{2,1,0:T(8,128)(2,1)S(1)} %pad_maximum_fusion.2), channel_id=1, source_target_pairs={{0,8},{1,9},{2,10},{3,11},{4,12},{5,13},{6,14},{7,15},{8,0},{9,1},... | collective-permute-start | bytes 1572872 | tf_op jit(solution)/shard_map/ppermute | solution.py:19
  45.3 74.0 %collective-permute-start.4 = (bf16[16,64,512]{2,1,0:T(8,128)(2,1)}, bf16[16,64,512]{2,1,0:T(8,128)(2,1)}, u32[]{:S(2)}, u32[]{:S(2)}) collective-permute-start(bf16[16,64,512]{2,1,0:T(8,128)(2,1)} %pad_maximum_fusion.1), channel_id=1, source_target_pairs={{0,16},{1,17},{2,18},{3,19},{4,20},{5,21},{6,22},{7,23},{8,24},{9,... | collective-permute-start | bytes 3145736 | tf_op jit(solution)/shard_map/ppermute | solution.py:19
